TPU v7x, 32 devices: a whole 2x2x4 slice. The times are simulated.
32 devices in a mesh: lang: 4 (over x, core), dp: 8 (over z, y).
Axes of the slice: x: 2, y: 2, z: 4, core: 2. Of those that a mesh axis runs over, the one named last changes fastest.
Arguments:
- src_emb: bfloat16 [4096, 768], P(('lang', 'dp')), may hold values from -6 to 6
- tgt_emb: bfloat16 [4, 1024, 768], P(None, ('lang', 'dp')), may hold values from -6 to 6
- slot_group: int32 [4], replicated, may hold values from 0 to 3, each once
- counts: int32 [4], replicated, may hold values from 256 to 1024, as said below
- align: int32 [4, 1024], P('lang'), may hold values from 0 to 1023, each once within a row
- pair_weight: float32 [4], replicated, may hold values from 4 to 40
Outputs:
- grad_src: bfloat16 [4096, 768], P(('lang', 'dp'))
- grad_tgt: bfloat16 [4, 1024, 768], P(None, ('lang', 'dp'))
- pair_loss: float32 [4], P('lang')
Inputs may be any that keep to these rules, and one draw needn't show every extreme that they name: `counts`: at least one pair has all 1024 sentences live. `align`: each row is a permutation.
All inputs are finite; a program needn't handle non-finite values.
Results may differ from a plain program's by a relative error of at most 0.0057.
Values may be sent and summed in bfloat16 or wider, within the bound.
No kernel may reach another device: no remote copies, remote signals or barrier semaphores. Data moves between devices by JAX's collectives and lax.ppermute only.
A program may use at most 64 MiB of HBM per device.

v0:
```python
import math
import jax
import jax.numpy as jnp
from jax import lax
from jax.sharding import PartitionSpec as P

MARGIN = 0.3
LOW_FILL = -1e30
BLOCK_BYTES = 8 * 1024 * 1024


def target_index(col_count, row_count, per_slot, data_size):
    position = jnp.arange(col_count, dtype=jnp.int32)
    source = position // row_count
    within = position % row_count
    return (within // per_slot * data_size + source) * per_slot + within % per_slot


def scores_of(x_rows, y_rows, pos_mask, inv_root):
    raw_dot = lax.dot_general(
        x_rows, y_rows, (((1,), (1,)), ((), ())), preferred_element_type=jnp.float32
    )
    return raw_dot * inv_root - MARGIN * pos_mask.astype(jnp.float32)


def block_stats(scores_f, is_pos, row_live, col_ok):
    row_max = jnp.max(jnp.where(col_ok[None, :], scores_f, LOW_FILL), axis=1)
    row_sum = jnp.sum(jnp.where(col_ok[None, :], jnp.exp(scores_f - row_max[:, None]), 0.0), axis=1)
    row_lse = row_max + jnp.log(row_sum + (1.0 - row_live.astype(jnp.float32)))
    pos_score = jnp.sum(jnp.where(is_pos, scores_f, 0.0), axis=1)
    col_max = jnp.max(jnp.where(row_live[:, None], scores_f, LOW_FILL), axis=0)
    col_sum = jnp.sum(
        jnp.where(row_live[:, None], jnp.exp(scores_f - col_max[None, :]), 0.0), axis=0
    )
    return (row_lse, pos_score, col_max, col_sum)


def grad_of(scores_f, is_pos, row_ok, col_ok, row_lse, col_lse, weight):
    both_live = row_ok[:, None] & col_ok[None, :]
    by_row = jnp.where(both_live, jnp.exp(scores_f - row_lse[:, None]), 0.0)
    by_col = jnp.where(both_live, jnp.exp(scores_f - col_lse[None, :]), 0.0)
    pos_hit = (is_pos & row_ok[:, None]).astype(jnp.float32)
    return (weight * (by_row + by_col - 2.0 * pos_hit)).astype(jnp.bfloat16)


def per_device(src_emb, tgt_emb, slot_group, counts, align, pair_weight):
    lang_size = lax.axis_size("lang")
    data_size = lax.axis_size("dp")
    row_count, emb_width = src_emb.shape
    per_slot = tgt_emb.shape[1]
    pair_rows = row_count * data_size
    inv_root = 1.0 / math.sqrt(emb_width)
    group_index = lax.axis_index("lang")
    shard_index = lax.axis_index("dp")
    slot_ids = jnp.arange(lang_size, dtype=jnp.int32)
    slot_of_group = jnp.zeros((lang_size,), jnp.int32).at[slot_group].set(slot_ids)
    ordered = tgt_emb[slot_of_group]
    arrived = lax.all_to_all(ordered, "lang", split_axis=0, concat_axis=1, tiled=True)
    partner = arrived[0]
    live_count = counts[group_index]
    weight = pair_weight[group_index]
    pair_align = align[0]
    all_rows = jnp.arange(pair_rows, dtype=jnp.int32)
    row_live = all_rows < live_count
    col_live_global = (
        jnp.zeros((pair_rows,), jnp.int32).at[pair_align].set(row_live.astype(jnp.int32))
    )
    perm = target_index(pair_rows, row_count, per_slot, data_size)
    col_live = col_live_global[perm] > 0
    x_all = lax.all_gather(src_emb, "dp", axis=0, tiled=True)
    y_all = lax.all_gather(partner, "dp", axis=0, tiled=True)
    block = max(1, min(pair_rows, BLOCK_BYTES // (4 * pair_rows)))
    steps = pair_rows // block
    if steps == 1:
        is_pos = perm[None, :] == pair_align[:, None]
        scores_f = scores_of(x_all, y_all, is_pos, inv_root)
        row_lse, pos_score, col_max, col_sum = block_stats(scores_f, is_pos, row_live, col_live)
    else:

        def one_block(k, carry):
            row_lse, pos_score, col_max, col_sum = carry
            start = k * block
            x_blk = lax.dynamic_slice_in_dim(x_all, start, block)
            a_blk = lax.dynamic_slice_in_dim(pair_align, start, block)
            r_blk = lax.dynamic_slice_in_dim(row_live, start, block)
            is_pos = perm[None, :] == a_blk[:, None]
            s_blk = scores_of(x_blk, y_all, is_pos, inv_root)
            b_lse, b_pos, b_max, b_sum = block_stats(s_blk, is_pos, r_blk, col_live)
            top = jnp.maximum(col_max, b_max)
            col_sum = col_sum * jnp.exp(col_max - top) + b_sum * jnp.exp(b_max - top)
            row_lse = lax.dynamic_update_slice_in_dim(row_lse, b_lse, start, 0)
            pos_score = lax.dynamic_update_slice_in_dim(pos_score, b_pos, start, 0)
            return (row_lse, pos_score, top, col_sum)

        zeros = jnp.zeros((pair_rows,), jnp.float32)
        init = (zeros, zeros, jnp.full((pair_rows,), LOW_FILL, jnp.float32), zeros)
        row_lse, pos_score, col_max, col_sum = lax.fori_loop(0, steps, one_block, init)
    col_lse = col_max + jnp.log(col_sum + (1.0 - col_live.astype(jnp.float32)))
    row_f = row_live.astype(jnp.float32)
    col_f = col_live.astype(jnp.float32)
    total = jnp.sum(row_f * (row_lse - 2.0 * pos_score)) + jnp.sum(col_f * col_lse)
    pair_loss = (total / live_count.astype(jnp.float32)).reshape(1)
    mine = shard_index * row_count
    x_my = lax.dynamic_slice_in_dim(x_all, mine, row_count)
    a_my = lax.dynamic_slice_in_dim(pair_align, mine, row_count)
    r_my = lax.dynamic_slice_in_dim(row_live, mine, row_count)
    lse_my = lax.dynamic_slice_in_dim(row_lse, mine, row_count)
    pos_rows = perm[None, :] == a_my[:, None]
    s_rows = scores_of(x_my, y_all, pos_rows, inv_root)
    g_rows = grad_of(s_rows, pos_rows, r_my, col_live, lse_my, col_lse, weight)
    grad_src = (jnp.dot(g_rows, y_all, preferred_element_type=jnp.float32) * inv_root).astype(
        jnp.bfloat16
    )
    p_my = lax.dynamic_slice_in_dim(perm, mine, row_count)
    c_my = lax.dynamic_slice_in_dim(col_live, mine, row_count)
    clse_my = lax.dynamic_slice_in_dim(col_lse, mine, row_count)
    pos_cols = p_my[None, :] == pair_align[:, None]
    s_cols = scores_of(x_all, partner, pos_cols, inv_root)
    g_cols = grad_of(s_cols, pos_cols, row_live, c_my, row_lse, clse_my, weight)
    own_terms = lax.dot_general(
        g_cols, x_all, (((0,), (0,)), ((), ())), preferred_element_type=jnp.float32
    )
    grad_local = (own_terms * inv_root).astype(jnp.bfloat16)
    returned = lax.all_to_all(
        grad_local.reshape(1, row_count, emb_width), "lang", split_axis=1, concat_axis=0, tiled=True
    )
    grad_tgt = returned[slot_group]
    return (grad_src, grad_tgt, pair_loss)


def solution(mesh):
    in_specs = (
        P(("lang", "dp"), None),
        P(None, ("lang", "dp"), None),
        P(),
        P(),
        P("lang", None),
        P(),
    )
    out_specs = (P(("lang", "dp"), None), P(None, ("lang", "dp"), None), P("lang"))
    return jax.shard_map(
        per_device, mesh=mesh, in_specs=in_specs, out_specs=out_specs, check_vma=False
    )
```

profile of v0, /device:TPU:0, one launch (start us, length us, event | category | flops | bytes accessed | tf_op | source)
XLA Modules:
  0.0 133.8 jit_solution(15715575883117667560)
XLA Ops:
  7.2 0.7 all-gather.3.cloned.1.call-update
  7.9 0.0 all-gather.5.cloned.1.call-start
  8.0 0.7 compare_select_fusion.10
  8.6 0.6 scatter_custom_fusion.1
  9.3 0.6 gather_fusion.1
  9.8 9.4 %all_to_all.21 = bf16[4,32,768]{2,1,0:T(8,128)(2,1)} all-to-all(bf16[4,32,768]{2,1,0:T(8,128)(2,1)S(1)} %gather_fusion.1), channel_id=1, replica_groups=mesh['lang'=4,'dp'=8] {'lang'}, dimensions={0} | all-to-all | bytes 393216 | tf_op jit(solution)/shard_map/all_to_all | solution.py:58
  19.3 1.2 dynamic_slice.28
  21.2 0.7 fusion.61
  21.9 0.7 compare_select_fusion.5
  22.6 4.3 %scatter_custom_fusion = s32[1024]{0:T(1024)S(1)} fusion(s32[1024]{0:T(1024)S(1)} %bitcast.44, s32[1024]{0:T(1024)S(1)} %fusion.61, s32[]{:T(128)} %constant.94.clone.1), kind=kCustom, calls=%fused_computation.116 | custom fusion | bytes 4100 | tf_op jit(solution)/shard_map/scatter | solution.py:66
  26.9 4.5 %gather_fusion = s32[1024]{0:T(1024)S(1)} fusion(s32[1024]{0:T(1024)S(1)} %scatter_custom_fusion, s32[1024]{0:T(1024)S(1)} %broadcast_clamp_fusion), kind=kCustom, calls=%fused_computation | custom fusion | bytes 12288 | tf_op jit(solution)/shard_map/gather | solution.py:69
  31.5 0.1 dynamic_slice.33
  31.6 0.1 dynamic_slice.34
  31.7 0.6 dynamic_slice.27
  32.3 0.6 iota_compare_fusion
  32.9 0.1 dynamic_slice.29
  33.0 24.2 %all-gather.3.cloned.1.call-done = bf16[1024,768]{1,0:T(8,128)(2,1)} async-done(((bf16[128,768]{1,0:T(8,128)(2,1)}), bf16[1024,768]{1,0:T(8,128)(2,1)}) %all-gather.3.cloned.1.call-update) | async-done | bytes 1572880 | tf_op jit(solution)/shard_map/all_gather | solution.py:70
  57.2 44.8 %all-gather.5.cloned.1.call-done = bf16[1024,768]{1,0:T(8,128)(2,1)} async-done(((bf16[128,768]{1,0:T(8,128)(2,1)}), bf16[1024,768]{1,0:T(8,128)(2,1)}) %all-gather.5.cloned.1.call-update) | async-done | bytes 1572880 | tf_op jit(solution)/shard_map/all_gather | solution.py:71
  101.9 4.5 %select_reduce_fusion.3 = (f32[1024]{0:T(1024)S(1)}, f32[1024]{0:T(1024)S(1)}, f32[1024,1024]{0,1:T(8,128)S(1)}) fusion(pred[1024]{0:T(1024)(128)(4,1)S(1)} %broadcast_compare_fusion, pred[1024]{0:T(1024)(128)(4,1)S(1)} %iota_compare_fusion, s32[1024]{0:T(1024)S(1)} %bitcast.40, s32[1024]{0:T(1024)S(1)} %fusion.50, ...), kind=kOutput, calls=%fused_computation.12 | convolution fusion | flops 1618999296 | bytes 7358464 | tf_op jit(solution)/shard_map/dot_general | solution.py:20
  106.5 2.5 %fusion.1 = (f32[1024]{0:T(1024)S(1)}, f32[1024]{0:T(1024)S(1)}, f32[1024]{0:T(1024)S(1)}) fusion(f32[1024,1024]{0,1:T(8,128)S(1)} %get-tuple-element.12, s32[1024]{0:T(1024)S(1)} %bitcast.41, s32[1024]{0:T(1024)S(1)} %fusion.50, f32[1024]{0:T(1024)S(1)} %get-tuple-element.7, pred[1024]{0:T(1024)(128)(4,1)S(1)} %iota_compare_fusion, ...), kind=kLoop, calls=%fused_computation.8 | loop fusion | flops 9434112 | bytes 4225024 | tf_op jit(solution)/shard_map/reduce_sum | solution.py:30
  108.9 1.3 select_reduce_fusion.4
  110.2 0.1 dynamic_slice.35
  110.3 0.1 dynamic_slice.32
  110.4 1.7 %fusion.7 = bf16[1,128,768]{2,1,0:T(8,128)(2,1)S(1)} fusion(bf16[1024,768]{1,0:T(8,128)(2,1)S(1)} %copy-done.3, bf16[128,768]{1,0:T(8,128)(2,1)S(1)} %bitcast.38, f32[128]{0:T(128)S(1)} %dynamic_slice.35, f32[1024]{0:T(1024)S(1)} %get-tuple-element.14, s32[1024]{0:T(1024)S(1)} %bitcast.42, f32[]{:T(128)} %bitcast, s32[128]{0:T(128)S(1)} %dynamic_slice.34, ...), kind=kOutput, calls=%fused_computation.22 | convolution fusion | flops 404815872 | bytes 1976452 | tf_op jit(solution)/shard_map/dot_general | solution.py:120
  112.1 0.3 copy.13
  112.4 0.5 broadcast.415
  112.9 1.8 %reduce = bf16[128,768]{1,0:T(8,128)(2,1)S(1)} reduce(bf16[128,1,768]{2,1,0:T(2,128)(2,1)S(1)} %bitcast.36, bf16[]{:T(256)} %broadcast.415), dimensions={1}, to_apply=%bitcast.34.reduce_sub_computation | reduce | bytes 393218
  114.7 0.7 reshape.320
  115.5 3.4 %all-to-all-start.1 = ((bf16[4,2,12288]{2,1,0:T(2,128)(2,1)}), bf16[4,2,12288]{2,1,0:T(2,128)(2,1)S(1)}, u32[]{:S(2)}, u32[]{:S(2)}) async-start(bf16[4,2,12288]{2,1,0:T(2,128)(2,1)} %reshape.320), calls=%async_computation.1 | async-start | bytes 393216 | tf_op jit(solution)/shard_map/all_to_all | solution.py:124
  118.8 4.2 %fusion.5 = bf16[128,768]{1,0:T(8,128)(2,1)} fusion(bf16[1024,768]{1,0:T(8,128)(2,1)} %all-gather.5.cloned.1.call-done, f32[1024]{0:T(1024)S(1)} %get-tuple-element.9, f32[128]{0:T(128)S(1)} %dynamic_slice.32, s32[1024]{0:T(1024)S(1)} %fusion.50, f32[]{:T(128)} %bitcast, s32[128]{0:T(128)S(1)} %dynamic-slice_bitcast_fusion, ...), kind=kOutput, calls=%fused_computation.20 | convolution fusion | flops 404815872 | bytes 3550212 | tf_op jit(solution)/shard_map/dot_general | solution.py:111
  124.4 0.2 reshape.321
  124.6 1.2 gather_fusion.2
  (23 shorter events, 0.2 us)
Async XLA Ops:
  7.2 2.1 %copy-start = (bf16[4,32,768]{2,1,0:T(8,128)(2,1)S(1)}, bf16[4,32,768]{2,1,0:T(8,128)(2,1)}, u32[]{:S(2)}) copy-start(bf16[4,32,768]{2,1,0:T(8,128)(2,1)} %param.7) | copy-start | bytes 589828
  7.2 25.8 %copy-start.2 = (s32[1,1024]{1,0:T(1,128)S(1)}, s32[1,1024]{1,0:T(1,128)}, u32[]{:S(2)}) copy-start(s32[1,1024]{1,0:T(1,128)} %param.10) | copy-start | bytes 12292
  7.2 24.5 %copy-start.4 = (f32[4]{0:T(128)S(1)}, f32[4]{0:T(128)}, u32[]{:S(2)}) copy-start(f32[4]{0:T(128)} %param.11) | copy-start | bytes 52
  7.2 50.0 %all-gather.3.cloned.1.call-start = ((), (), s32[]{:S(2)}) async-start(), calls=%async_computation.2 | async-start | bytes 1769472 | tf_op jit(solution)/shard_map/all_gather | solution.py:70
  7.9 94.0 %all-gather.5.cloned.1.call-start = ((), (), s32[]{:S(2)}) async-start(), calls=%async_computation.3 | async-start | bytes 1769472 | tf_op jit(solution)/shard_map/all_gather | solution.py:71
  106.4 4.0 %copy-start.1 = (bf16[4,32,768]{2,1,0:T(8,128)(2,1)S(1)}, bf16[4,32,768]{2,1,0:T(8,128)(2,1)}, u32[]{:S(2)}) copy-start(bf16[4,32,768]{2,1,0:T(8,128)(2,1)} %all_to_all.21) | copy-start | bytes 589828
  106.4 3.9 %copy-start.3 = (bf16[1024,768]{1,0:T(8,128)(2,1)S(1)}, bf16[1024,768]{1,0:T(8,128)(2,1)}, u32[]{:S(2)}) copy-start(bf16[1024,768]{1,0:T(8,128)(2,1)} %all-gather.3.cloned.1.call-done) | copy-start | bytes 4718596
  115.5 8.9 %all-to-all-start.1 = ((bf16[4,2,12288]{2,1,0:T(2,128)(2,1)}), bf16[4,2,12288]{2,1,0:T(2,128)(2,1)S(1)}, u32[]{:S(2)}, u32[]{:S(2)}) async-start(bf16[4,2,12288]{2,1,0:T(2,128)(2,1)} %reshape.320), calls=%async_computation.1 | async-start | bytes 393216 | tf_op jit(solution)/shard_map/all_to_all | solution.py:124
Sparse Core Ops, SparseCore 0:
  10.2 46.9 all-gather.2
  59.4 42.5 all-gather.4
where the time goes:
time: 134 us
  waiting for transfers between devices  69.6 us (52%)
  between operations  17.3 us (13%)
  local copies, waits for them, and re-layouts  15.2 us (11%)
  matrix products  10.4 us (8%)
  blocking collectives  9.44 us (7%)
  other arithmetic  8.34 us (6%)
  starting transfers between devices  3.44 us (3%)
    all_gather x1, waiting for transfers between devices, per_device(): y_all = lax.all_gather(partner, 'dp', axis=0, tiled=True)  44.8 us
    all_gather x1, waiting for transfers between devices, per_device(): x_all = lax.all_gather(src_emb, 'dp', axis=0, tiled=True)  24.2 us
    all_to_all x1, blocking collectives, per_device(): lax.all_to_all(ordered, 'lang', split_axis=0, concat_axis=1, tiled=True)  9.44 us
    gather x1, local copies, waits for them, and re-layouts, per_device(): col_live = col_live_global[perm] > 0  4.53 us
    dot_general x1, matrix products, scores_of(): lax.dot_general(x_rows, y_rows, (((1,), (1,)), ((), ())), preferred_eleme...  4.5 us
    scatter x1, local copies, waits for them, and re-layouts, per_device(): jnp.zeros((pair_rows,), jnp.int32).at[pair_align]  4.31 us
    dot_general x1, matrix products, per_device(): jnp.dot(g_rows, y_all, preferred_element_type=jnp.float32) * inv_root  4.24 us
    all_to_all x1, starting transfers between devices, per_device(): lax.all_to_all(grad_local.reshape(1, row_count, emb_width), 'lang', split...  3.37 us
  transfers between devices with their start and end apart: 3, of which 2 were waited for; matrix products, arithmetic and copies ran while one was open for 14% of the time, Pallas kernels for 0%

commit v1 on v0

--- a/solution.py
+++ b/solution.py
@@ -67,8 +67,15 @@
     )
     perm = target_index(pair_rows, row_count, per_slot, data_size)
     col_live = col_live_global[perm] > 0
-    x_all = lax.all_gather(src_emb, "dp", axis=0, tiled=True)
-    y_all = lax.all_gather(partner, "dp", axis=0, tiled=True)
+
+    def make_the_floor(axis_name, tile_in, a0):
+        return jnp.split(
+            lax.all_gather(jnp.concatenate([tile_in, a0], axis=1), axis_name, axis=0, tiled=True),
+            [tile_in.shape[1]],
+            axis=1,
+        )
+
+    x_all, y_all = make_the_floor("dp", src_emb, partner)
     block = max(1, min(pair_rows, BLOCK_BYTES // (4 * pair_rows)))
     steps = pair_rows // block
     if steps == 1:

time: 134 us -> 119 us (0.89)
  waiting for transfers between devices: 69.6 us -> 44.7 us
  local copies, waits for them, and re-layouts: 15.2 us -> 20.9 us
  other arithmetic: 8.34 us -> 10.9 us
    all_gather x2 -> x1, waiting for transfers between devices: 68.9 us -> 44.7 us  [make_the_floor(): lax.all_gather(jnp.concatenate([tile_in, a0], axis=1), axis_name, axis=0,...]
    concatenate x0 -> x1, other arithmetic: none -> 1.7 us  [make_the_floor(): jnp.concatenate([tile_in, a0], axis=1)]
    split x0 -> x1, local copies, waits for them, and re-layouts: none -> 1.51 us  [make_the_floor(): jnp.split(lax.all_gather(jnp.concatenate([tile_in, a0], axis=1), axis_nam...]
    dot_general x1, matrix products: 1.68 us -> 3.12 us  [per_device(): lax.dot_general(g_cols, x_all, (((0,), (0,)), ((), ())), preferred_elemen...]
  transfers between devices with their start and end apart: 3 -> 2, of which waited for: 2 -> 1; matrix products, arithmetic and copies ran while one was open for 14% -> 18% of each run, Pallas kernels for 0% -> 0%
where the time goes in v1:
time: 119 us; the launch traced here: 118 us
  waiting for transfers between devices  44.7 us (38%)
  local copies, waits for them, and re-layouts  20.9 us (18%)
  between operations  17.4 us (15%)
  matrix products  11.6 us (10%)
  other arithmetic  10.9 us (9%)
  blocking collectives  9.34 us (8%)
  starting transfers between devices  3.4 us (3%)
    all_gather x1, waiting for transfers between devices, make_the_floor(): lax.all_gather(jnp.concatenate([tile_in, a0], axis=1), axis_name, axis=0,...  44.7 us
    all_to_all x1, blocking collectives, per_device(): lax.all_to_all(ordered, 'lang', split_axis=0, concat_axis=1, tiled=True)  9.34 us
    gather x1, local copies, waits for them, and re-layouts, per_device(): col_live = col_live_global[perm] > 0  4.53 us
    scatter x1, local copies, waits for them, and re-layouts, per_device(): jnp.zeros((pair_rows,), jnp.int32).at[pair_align]  4.31 us
    dot_general x1, matrix products, scores_of(): lax.dot_general(x_rows, y_rows, (((1,), (1,)), ((), ())), preferred_eleme...  4.25 us
    dot_general x1, matrix products, per_device(): jnp.dot(g_rows, y_all, preferred_element_type=jnp.float32) * inv_root  4.24 us
    all_to_all x1, starting transfers between devices, per_device(): lax.all_to_all(grad_local.reshape(1, row_count, emb_width), 'lang', split...  3.37 us
    reduce_sum x1, other arithmetic, block_stats(): pos_score = jnp.sum(jnp.where(is_pos, scores_f, 0.0), axis=1)  3.28 us
  transfers between devices with their start and end apart: 2, of which 1 were waited for; matrix products, arithmetic and copies ran while one was open for 18% of the time, Pallas kernels for 0%

profile of v1, /device:TPU:0, one launch (start us, length us, event | category | flops | bytes accessed | tf_op | source)
XLA Modules:
  0.0 118.3 jit_solution(16725916422620188701)
XLA Ops:
  7.2 0.7 compare_select_fusion.10
  8.0 0.6 scatter_custom_fusion.1
  8.6 0.6 gather_fusion.1
  9.2 9.3 %all_to_all.21 = bf16[4,32,768]{2,1,0:T(8,128)(2,1)S(1)} all-to-all(bf16[4,32,768]{2,1,0:T(8,128)(2,1)S(1)} %gather_fusion.1), channel_id=1, replica_groups=mesh['lang'=4,'dp'=8] {'lang'}, dimensions={0} | all-to-all | bytes 393216 | tf_op jit(solution)/shard_map/all_to_all | solution.py:58
  18.5 1.7 %pad_maximum_fusion = bf16[128,1536]{1,0:T(8,128)(2,1)} fusion(bf16[128,768]{1,0:T(8,128)(2,1)S(1)} %bitcast.21, bf16[128,768]{1,0:T(8,128)(2,1)} %param.6), kind=kLoop, calls=%fused_computation.41 | loop fusion | flops 786432 | bytes 786432 | tf_op jit(solution)/shard_map/concatenate | solution.py:73
  20.2 1.2 %dynamic_slice.28 = s32[1]{0:T(128)} dynamic-slice(s32[4]{0:T(128)} %param.9, s32[]{:T(128)S(6)} %select_n.159), dynamic_slice_sizes={1} | dynamic-slice | bytes 12 | tf_op jit(solution)/shard_map/dynamic_slice | solution.py:60
  22.1 0.6 fusion.69
  22.8 0.7 compare_select_fusion.5
  23.5 4.3 %scatter_custom_fusion = s32[1024]{0:T(1024)S(1)} fusion(s32[1024]{0:T(1024)S(1)} %bitcast.28, s32[1024]{0:T(1024)S(1)} %fusion.69, s32[]{:T(128)} %constant.94.clone.1), kind=kCustom, calls=%fused_computation.119 | custom fusion | bytes 4100 | tf_op jit(solution)/shard_map/scatter | solution.py:66
  27.8 4.5 %gather_fusion = s32[1024]{0:T(1024)S(1)} fusion(s32[1024]{0:T(1024)S(1)} %scatter_custom_fusion, s32[1024]{0:T(1024)S(1)} %broadcast_clamp_fusion), kind=kCustom, calls=%fused_computation | custom fusion | bytes 12288 | tf_op jit(solution)/shard_map/gather | solution.py:69
  32.4 0.6 dynamic_slice.33
  33.0 0.6 dynamic_slice.34
  33.6 0.5 dynamic_slice.27
  34.2 0.6 iota_compare_fusion
  34.9 0.6 dynamic_slice.29
  35.5 0.5 dynamic-slice_bitcast_fusion
  36.0 44.7 %all-gather.2.cloned.1.call-done = bf16[1024,1536]{1,0:T(8,128)(2,1)} async-done(((bf16[128,1536]{1,0:T(8,128)(2,1)}), bf16[1024,1536]{1,0:T(8,128)(2,1)}) %all-gather.2.cloned.1.call-update) | async-done | bytes 3145744 | tf_op jit(solution)/shard_map/all_gather | solution.py:73
  80.7 4.3 %select_reduce_fusion.3 = (f32[1024]{0:T(1024)S(1)}, f32[1024]{0:T(1024)S(1)}, f32[1024,1024]{0,1:T(8,128)S(1)}) fusion(pred[1024]{0:T(1024)(128)(4,1)S(1)} %broadcast_compare_fusion, pred[1024]{0:T(1024)(128)(4,1)S(1)} %iota_compare_fusion, s32[1024]{0:T(1024)S(1)} %bitcast.24, s32[1024]{0:T(1024)S(1)} %fusion.58, ...), kind=kOutput, calls=%fused_computation.12 | convolution fusion | flops 1618999296 | bytes 7358464 | tf_op jit(solution)/shard_map/dot_general | solution.py:20
  85.0 3.3 %fusion.1 = (f32[1024]{0:T(1024)S(1)}, f32[1024]{0:T(1024)S(1)}, f32[1024]{0:T(1024)S(1)}) fusion(f32[1024,1024]{0,1:T(8,128)S(1)} %get-tuple-element.12, s32[1024]{0:T(1024)S(1)} %bitcast.25, s32[1024]{0:T(1024)S(1)} %fusion.58, f32[1024]{0:T(1024)S(1)} %get-tuple-element.7, pred[1024]{0:T(1024)(128)(4,1)} %copy-done.8, f32[1024]{0:T(1024)S(1)} %get-tuple-element.6, ...), kind=kLoop, calls=%fused_computation.8 | loop fusion | flops 9434112 | bytes 4225024 | tf_op jit(solution)/shard_map/reduce_sum | solution.py:30
  88.3 1.3 %select_reduce_fusion.4 = (f32[]{:T(128)}, f32[1024]{0:T(1024)S(1)}, f32[]{:T(128)}, f32[1024]{0:T(1024)S(1)}) fusion(f32[1024]{0:T(1024)S(1)} %get-tuple-element.7, f32[1024]{0:T(1024)S(1)} %get-tuple-element.4, f32[1024]{0:T(1024)S(1)} %get-tuple-element.3, f32[1024]{0:T(1024)S(1)} %get-tuple-element.6, f32[1024]{0:T(1024)S(1)} %get-tuple-element.5, ...), kind=kLoop, calls=%fused_computation.105 | loop fusion | flops 16382 | bytes 32780 | tf_op jit(solution)/shard_map/reduce_sum | solution.py:108
  89.6 0.6 copy-done.5
  90.3 0.6 dynamic_slice.32
  90.9 3.1 %fusion.11 = bf16[1,128,768]{2,1,0:T(8,128)(2,1)} fusion(bf16[128,768]{1,0:T(8,128)(2,1)S(1)} %bitcast.22, f32[128]{0:T(128)S(1)} %dynamic_slice.35, f32[1024]{0:T(1024)} %copy-done.7, s32[128]{0:T(128)} %dynamic_slice.34, f32[]{:T(128)} %bitcast, s32[1024]{0:T(1024)S(1)} %bitcast.26, pred[128]{0:T(512)(128)(4,1)} %dynamic_slice.33, ...), kind=kOutput, calls=%fused_computation.24 | convolution fusion | flops 404815872 | bytes 3549316 | tf_op jit(solution)/shard_map/dot_general | solution.py:127
  94.0 1.2 %copy.13 = bf16[1,128,768]{2,0,1:T(2,128)(2,1)S(1)} copy(bf16[1,128,768]{2,1,0:T(8,128)(2,1)} %fusion.11) | data formatting | bytes 393216 | tf_op jit(solution)/shard_map/reshape | solution.py:132
  95.2 0.5 broadcast.411
  95.8 1.8 %reduce = bf16[128,768]{1,0:T(8,128)(2,1)S(1)} reduce(bf16[128,1,768]{2,1,0:T(2,128)(2,1)S(1)} %bitcast.20, bf16[]{:T(256)} %broadcast.411), dimensions={1}, to_apply=%bitcast.18.reduce_sub_computation | reduce | bytes 393218
  97.6 0.7 reshape.320
  98.3 3.4 %all-to-all-start.1 = ((bf16[4,2,12288]{2,1,0:T(2,128)(2,1)}), bf16[4,2,12288]{2,1,0:T(2,128)(2,1)S(1)}, u32[]{:S(2)}, u32[]{:S(2)}) async-start(bf16[4,2,12288]{2,1,0:T(2,128)(2,1)} %reshape.320), calls=%async_computation.1 | async-start | bytes 393216 | tf_op jit(solution)/shard_map/all_to_all | solution.py:131
  101.7 1.5 %split.8 = bf16[1024,768]{1,0:T(8,128)(2,1)S(1)} slice(bf16[1024,1536]{1,0:T(8,128)(2,1)} %all-gather.2.cloned.1.call-done), slice={[0:1024], [0:768]} | slice | bytes 3145728 | tf_op jit(solution)/shard_map/split | solution.py:72
  103.3 4.2 %fusion.7 = bf16[128,768]{1,0:T(8,128)(2,1)} fusion(bf16[1024,1536]{1,0:T(8,128)(2,1)} %all-gather.2.cloned.1.call-done, f32[1024]{0:T(1024)S(1)} %copy-done.6, f32[128]{0:T(128)S(1)} %copy-done.12, s32[1024]{0:T(1024)S(1)} %fusion.58, f32[]{:T(128)} %bitcast, s32[128]{0:T(128)S(1)} %copy-done.11, pred[1024]{0:T(1024)(128)(4,1)S(1)} %copy-done.4, ...), kind=kOutput, calls=%fused_computation.22 | convolution fusion | flops 404815872 | bytes 3549704 | tf_op jit(solution)/shard_map/dot_general | solution.py:118
  108.9 0.2 reshape.321
  109.1 1.2 %gather_fusion.2 = bf16[4,32,768]{2,1,0:T(8,128)(2,1)} fusion(bf16[4,32,768]{2,1,0:T(8,128)(2,1)S(1)} %bitcast.23, s32[1024]{0:T(1024)S(1)} %pad_clamp_fusion), kind=kCustom, calls=%fused_computation.2 | custom fusion | bytes 393232 | tf_op jit(solution)/shard_map/gather | solution.py:134
  (38 shorter events, 0.3 us)
Async XLA Ops:
  7.2 1.4 %copy-start = (bf16[4,32,768]{2,1,0:T(8,128)(2,1)S(1)}, bf16[4,32,768]{2,1,0:T(8,128)(2,1)}, u32[]{:S(2)}) copy-start(bf16[4,32,768]{2,1,0:T(8,128)(2,1)} %param.7) | copy-start | bytes 589828
  7.2 28.3 %copy-start.2 = (s32[1,1024]{1,0:T(1,128)S(1)}, s32[1,1024]{1,0:T(1,128)}, u32[]{:S(2)}) copy-start(s32[1,1024]{1,0:T(1,128)} %param.10) | copy-start | bytes 12292
  7.2 26.5 %copy-start.9 = (f32[4]{0:T(128)S(1)}, f32[4]{0:T(128)}, u32[]{:S(2)}) copy-start(f32[4]{0:T(128)} %param.11) | copy-start | bytes 52
  7.2 73.5 %all-gather.2.cloned.1.call-start = ((), (), s32[]{:S(2)}) async-start(), calls=%async_computation.2 | async-start | bytes 3538944 | tf_op jit(solution)/shard_map/all_gather | solution.py:73
  32.4 48.3 %copy-start.3 = (pred[1024]{0:T(1024)(128)(4,1)}, pred[1024]{0:T(1024)(128)(4,1)S(1)}, u32[]{:S(2)}) copy-start(pred[1024]{0:T(1024)(128)(4,1)S(1)} %broadcast_compare_fusion) | copy-start | bytes 3076
  34.9 45.9 %copy-start.8 = (pred[1024]{0:T(1024)(128)(4,1)}, pred[1024]{0:T(1024)(128)(4,1)S(1)}, u32[]{:S(2)}) copy-start(pred[1024]{0:T(1024)(128)(4,1)S(1)} %iota_compare_fusion) | copy-start | bytes 3076
  85.0 5.9 %copy-start.1 = (bf16[1024,1536]{1,0:T(8,128)(2,1)S(1)}, bf16[1024,1536]{1,0:T(8,128)(2,1)}, u32[]{:S(2)}) copy-start(bf16[1024,1536]{1,0:T(8,128)(2,1)} %all-gather.2.cloned.1.call-done) | copy-start | bytes 9437188
  89.6 0.6 copy-start.5
  89.6 0.7 copy-start.7
  94.0 9.3 %copy-start.4 = (pred[1024]{0:T(1024)(128)(4,1)S(1)}, pred[1024]{0:T(1024)(128)(4,1)}, u32[]{:S(2)}) copy-start(pred[1024]{0:T(1024)(128)(4,1)} %copy-done.3) | copy-start | bytes 3076
  94.0 9.3 %copy-start.6 = (f32[1024]{0:T(1024)S(1)}, f32[1024]{0:T(1024)}, u32[]{:S(2)}) copy-start(f32[1024]{0:T(1024)} %copy-done.5) | copy-start | bytes 12292
  94.0 9.3 %copy-start.10 = (pred[128]{0:T(512)(128)(4,1)S(1)}, pred[128]{0:T(512)(128)(4,1)}, u32[]{:S(2)}) copy-start(pred[128]{0:T(512)(128)(4,1)} %dynamic_slice.29) | copy-start | bytes 388
  94.0 9.3 %copy-start.11 = (s32[128]{0:T(128)S(1)}, s32[128]{0:T(128)}, u32[]{:S(2)}) copy-start(s32[128]{0:T(128)} %dynamic-slice_bitcast_fusion) | copy-start | bytes 1540
  94.0 9.3 %copy-start.12 = (f32[128]{0:T(128)S(1)}, f32[128]{0:T(128)}, u32[]{:S(2)}) copy-start(f32[128]{0:T(128)} %dynamic_slice.32) | copy-start | bytes 1540
  98.3 10.5 %all-to-all-start.1 = ((bf16[4,2,12288]{2,1,0:T(2,128)(2,1)}), bf16[4,2,12288]{2,1,0:T(2,128)(2,1)S(1)}, u32[]{:S(2)}, u32[]{:S(2)}) async-start(bf16[4,2,12288]{2,1,0:T(2,128)(2,1)} %reshape.320), calls=%async_computation.1 | async-start | bytes 393216 | tf_op jit(solution)/shard_map/all_to_all | solution.py:131
Sparse Core Ops, SparseCore 0:
  20.3 60.3 all-gather.1
